TPU v7x, 256 devices: a whole 4x4x8 slice. The times are simulated.
256 devices in a mesh: row: 32 (over z, y), col: 8 (over x, core).
Axes of the slice: x: 4, y: 4, z: 8, core: 2. Of those that a mesh axis runs over, the one named last changes fastest.
Arguments:
- saved_input: bfloat16 [1024, 49152], P('col', 'row'), may hold values from -6 to 6
- out_grad: bfloat16 [1024, 12288], P('row', 'col'), may hold values from -0.75 to 0.75
- weight: bfloat16 [49152, 12288], P('row', 'col'), may hold values from -0.625 to 0.625
Outputs:
- in_grad: bfloat16 [1024, 49152], P('col', 'row')
- weight_grad: bfloat16 [49152, 12288], P('row', 'col')
All inputs are finite; a program needn't handle non-finite values.
Results may differ from a plain program's by a relative error of at most 0.0051.
Values may be sent and summed in bfloat16 or wider, within the bound.
No kernel may reach another device: no remote copies, remote signals or barrier semaphores. Data moves between devices by JAX's collectives and lax.ppermute only.
A program may use at most 64 MiB of HBM per device.

v0:
```python
import math
import jax
import jax.numpy as jnp
from jax import lax
from jax.sharding import PartitionSpec as P


def gelu_parts(values):
    coeff = math.sqrt(2.0 / math.pi)
    inner = jnp.tanh(coeff * (values + 0.044715 * values * values * values))
    gelu_value = 0.5 * values * (1.0 + inner)
    gelu_slope = 0.5 * (1.0 + inner) + 0.5 * values * (1.0 - inner * inner) * coeff * (
        1.0 + 3.0 * 0.044715 * values * values
    )
    return (gelu_value, gelu_slope)


def per_device(saved_input, out_grad, weight):
    grad_all = lax.all_gather(out_grad, "row", axis=0, tiled=True)
    saved_all = lax.all_gather(saved_input, "col", axis=0, tiled=True)
    gelu_value, unused_slope = gelu_parts(saved_all.astype(jnp.float32))
    hidden = gelu_value.astype(jnp.bfloat16)
    weight_grad = lax.dot_general(
        hidden, grad_all, (((0,), (0,)), ((), ())), preferred_element_type=jnp.float32
    ).astype(jnp.bfloat16)
    back = lax.psum_scatter(
        lax.dot_general(
            grad_all, weight, (((1,), (1,)), ((), ())), preferred_element_type=jnp.float32
        ),
        "col",
        scatter_dimension=0,
        tiled=True,
    )
    unused_value, own_slope = gelu_parts(saved_input.astype(jnp.float32))
    in_grad = (back * own_slope).astype(jnp.bfloat16)
    return (in_grad, weight_grad)


def solution(mesh):
    in_specs = (P("col", "row"), P("row", "col"), P("row", "col"))
    out_specs = (P("col", "row"), P("row", "col"))
    return jax.shard_map(
        per_device, mesh=mesh, in_specs=in_specs, out_specs=out_specs, check_vma=False
    )
```

profile of v0, /device:TPU:1, one launch (start us, length us, event | category | flops | bytes accessed | tf_op | source)
XLA Modules:
  0.0 178.5 jit_solution(13680003618552402031)
XLA Ops:
  7.2 0.0 all-gather.3.cloned.1.call-start
  7.2 0.7 all-gather.3.cloned.1.call-update
  7.9 0.0 all-gather.5.cloned.1.call-start
  7.9 0.7 all-gather.5.cloned.1.call-update
  8.6 0.0 reduce-scatter.2.cloned.1.call-start
  8.7 81.3 %all-gather.3.cloned.1.call-done = bf16[1024,1536]{1,0:T(8,128)(2,1)} async-done(((bf16[32,1536]{1,0:T(8,128)(2,1)}), bf16[1024,1536]{1,0:T(8,128)(2,1)}) %all-gather.3.cloned.1.call-update) | async-done | bytes 3145744 | tf_op jit(solution)/shard_map/all_gather | solution.py:19
  90.0 9.8 %fusion.23 = f32[1024,1536]{1,0:T(8,128)} fusion(bf16[1024,1536]{1,0:T(8,128)(2,1)} %all-gather.3.cloned.1.call-done, bf16[1536,1536]{1,0:T(8,128)(2,1)} %param.5), kind=kOutput, calls=%fused_computation.35 | convolution fusion | flops 4831838208 | bytes 14155776 | tf_op jit(solution)/shard_map/dot_general | solution.py:27
  99.7 0.0 copy-start.1
  99.7 0.0 reduce-scatter.2.cloned.1.call-update
  99.8 0.0 copy-start
  99.8 23.2 %all-gather.5.cloned.1.call-done = bf16[1024,1536]{1,0:T(8,128)(2,1)} async-done(((bf16[128,1536]{1,0:T(8,128)(2,1)}), bf16[1024,1536]{1,0:T(8,128)(2,1)}) %all-gather.5.cloned.1.call-update) | async-done | bytes 3145744 | tf_op jit(solution)/shard_map/all_gather | solution.py:20
  122.9 0.0 copy-done.1
  122.9 11.2 %convolution_convert_fusion = bf16[1536,1536]{1,0:T(8,128)(2,1)} fusion(bf16[1024,1536]{1,0:T(8,128)(2,1)S(1)} %copy-done.1, bf16[1024,1536]{1,0:T(8,128)(2,1)} %all-gather.5.cloned.1.call-done), kind=kOutput, calls=%fused_computation.5 | convolution fusion | flops 4849926144 | bytes 11010048 | tf_op jit(solution)/shard_map/dot_general | solution.py:23
  134.2 35.4 %reduce-scatter.2.cloned.1.call-done = f32[128,1536]{1,0:T(8,128)} async-done(((f32[1024,1536]{1,0:T(8,128)}), f32[128,1536]{1,0:T(8,128)}) %reduce-scatter.2.cloned.1.call-update) | async-done | bytes 786448 | tf_op jit(solution)/shard_map/reduce_scatter | solution.py:26
  169.6 0.0 copy-done
  169.6 2.4 %fusion.17 = bf16[128,1536]{1,0:T(8,128)(2,1)} fusion(f32[128,1536]{1,0:T(8,128)} %reduce-scatter.2.cloned.1.call-done, bf16[128,1536]{1,0:T(8,128)(2,1)S(1)} %copy-done), kind=kLoop, calls=%fused_computation.29 | loop fusion | flops 3932160 | bytes 1572864 | tf_op jit(solution)/shard_map/convert_element_type | solution.py:35
Async XLA Ops:
  7.2 82.8 %all-gather.3.cloned.1.call-start = ((), (), s32[]{:S(2)}) async-start(), calls=%async_computation.1 | async-start | bytes 3244032 | tf_op jit(solution)/shard_map/all_gather | solution.py:19
  7.9 115.0 %all-gather.5.cloned.1.call-start = ((), (), s32[]{:S(2)}) async-start(), calls=%async_computation.3 | async-start | bytes 3538944 | tf_op jit(solution)/shard_map/all_gather | solution.py:20
  8.6 161.0 %reduce-scatter.2.cloned.1.call-start = ((), (), s32[]{:S(2)}) async-start(), calls=%async_computation.2 | async-start | bytes 7077888 | tf_op jit(solution)/shard_map/reduce_scatter | solution.py:26
  99.7 23.2 %copy-start.1 = (bf16[1024,1536]{1,0:T(8,128)(2,1)S(1)}, bf16[1024,1536]{1,0:T(8,128)(2,1)}, u32[]{:S(2)}) copy-start(bf16[1024,1536]{1,0:T(8,128)(2,1)} %all-gather.3.cloned.1.call-done) | copy-start | bytes 9437188
  99.8 69.8 %copy-start = (bf16[128,1536]{1,0:T(8,128)(2,1)S(1)}, bf16[128,1536]{1,0:T(8,128)(2,1)}, u32[]{:S(2)}) copy-start(bf16[128,1536]{1,0:T(8,128)(2,1)} %param.3) | copy-start | bytes 1179652
Sparse Core Ops, SparseCore 0:
  10.5 79.3 all-gather.2
  91.8 31.1 all-gather.4
  125.5 44.0 reduce-scatter.1
where the time goes:
time: 179 us
  waiting for transfers between devices  141 us (79%)
  matrix products  21 us (12%)
  between operations  13.8 us (8%)
  other arithmetic  2.4 us (1%)
    all_gather x1, waiting for transfers between devices, per_device(): grad_all = lax.all_gather(out_grad, 'row', axis=0, tiled=True)  81.3 us
    reduce_scatter x1, waiting for transfers between devices, per_device(): lax.psum_scatter(lax.dot_general(grad_all, weight, (((1,), (1,)), ((), ()...  35.4 us
    all_gather x1, waiting for transfers between devices, per_device(): saved_all = lax.all_gather(saved_input, 'col', axis=0, tiled=True)  23.2 us
    dot_general x1, matrix products, per_device(): lax.dot_general(hidden, grad_all, (((0,), (0,)), ((), ())), preferred_ele...  11.2 us
    dot_general x1, matrix products, per_device(): lax.dot_general(grad_all, weight, (((1,), (1,)), ((), ())), preferred_ele...  9.78 us
  transfers between devices with their start and end apart: 3, of which 3 were waited for; matrix products, arithmetic and copies ran while one was open for 12% of the time, Pallas kernels for 0%

commit v1 on v0

--- a/solution.py
+++ b/solution.py
@@ -3,6 +3,19 @@
 import jax.numpy as jnp
 from jax import lax
 from jax.sharding import PartitionSpec as P
+
+
+def gather_around(shard, axis, dim):
+    ways = lax.axis_size(axis)
+    up = [(d, (d + 1) % ways) for d in range(ways)]
+    down = [(d, (d - 1) % ways) for d in range(ways)]
+    earlier, later = ([shard], [shard])
+    for _ in range(ways // 2):
+        earlier.append(lax.ppermute(earlier[-1], axis, up))
+    for _ in range((ways - 1) // 2):
+        later.append(lax.ppermute(later[-1], axis, down))
+    line = jnp.concatenate([*earlier[::-1], *later[1:]], axis=dim)
+    return jnp.roll(line, (lax.axis_index(axis) - ways // 2) * shard.shape[dim], axis=dim)
 
 
 def gelu_parts(values):
@@ -17,7 +30,7 @@
 
 def per_device(saved_input, out_grad, weight):
     grad_all = lax.all_gather(out_grad, "row", axis=0, tiled=True)
-    saved_all = lax.all_gather(saved_input, "col", axis=0, tiled=True)
+    saved_all = gather_around(saved_input, "col", 0)
     gelu_value, unused_slope = gelu_parts(saved_all.astype(jnp.float32))
     hidden = gelu_value.astype(jnp.bfloat16)
     weight_grad = lax.dot_general(

time: 179 us -> 168 us (0.939)
  waiting for transfers between devices: 141 us -> 116 us
  starting transfers between devices: 0.11 us -> 16 us
  matrix products: 21 us -> 17.1 us
    reduce_scatter x1, waiting for transfers between devices: 35.4 us -> 0.68 us  [per_device(): lax.psum_scatter(lax.dot_general(grad_all, weight, (((1,), (1,)), ((), ()...]
    ppermute x0 -> x7, waiting for transfers between devices: none -> 32.3 us  [the longest x4 27.6 us: gather_around(): earlier.append(lax.ppermute(earlier[-1], axis, up))]
    all_gather x1 -> x0, waiting for transfers between devices: 23.2 us -> none  [per_device(): saved_all = lax.all_gather(saved_input, 'col', axis=0, tiled=True)]
    ppermute x0 -> x7, starting transfers between devices: none -> 16 us  [the longest x4 13.1 us: gather_around(): earlier.append(lax.ppermute(earlier[-1], axis, up))]
    dot_general x1, matrix products: 11.2 us -> 7.36 us  [per_device(): lax.dot_general(hidden, grad_all, (((0,), (0,)), ((), ())), preferred_ele...]
  transfers between devices with their start and end apart: 3 -> 9, of which waited for: 3 -> 9; matrix products, arithmetic and copies ran while one was open for 12% -> 5% of each run, Pallas kernels for 0% -> 0%
where the time goes in v1:
time: 168 us; the launch traced here: 167 us
  waiting for transfers between devices  116 us (69%)
  matrix products  17.1 us (10%)
  starting transfers between devices  16 us (10%)
  between operations  14.2 us (8%)
  other arithmetic  2.4 us (1%)
    all_gather x1, waiting for transfers between devices, per_device(): grad_all = lax.all_gather(out_grad, 'row', axis=0, tiled=True)  82 us
    ppermute x4, waiting for transfers between devices, gather_around(): earlier.append(lax.ppermute(earlier[-1], axis, up))  27.6 us
    ppermute x4, starting transfers between devices, gather_around(): earlier.append(lax.ppermute(earlier[-1], axis, up))  13.1 us
    dot_general x1, matrix products, per_device(): lax.dot_general(grad_all, weight, (((1,), (1,)), ((), ())), preferred_ele...  9.76 us
    dot_general x1, matrix products, per_device(): lax.dot_general(hidden, grad_all, (((0,), (0,)), ((), ())), preferred_ele...  7.36 us
    ppermute x3, waiting for transfers between devices, gather_around(): later.append(lax.ppermute(later[-1], axis, down))  4.63 us
  transfers between devices with their start and end apart: 9, of which 9 were waited for; matrix products, arithmetic and copies ran while one was open for 5% of the time, Pallas kernels for 0%

profile of v1, /device:TPU:1, one launch (start us, length us, event | category | flops | bytes accessed | tf_op | source)
XLA Modules:
  0.0 166.8 jit_solution(2828911500196782964)
XLA Ops:
  7.2 0.0 all-gather.2.cloned.1.call-start
  7.2 0.7 all-gather.2.cloned.1.call-update
  7.9 0.0 reduce-scatter.2.cloned.1.call-start
  7.9 82.0 %all-gather.2.cloned.1.call-done = bf16[1024,1536]{1,0:T(8,128)(2,1)} async-done(((bf16[32,1536]{1,0:T(8,128)(2,1)}), bf16[1024,1536]{1,0:T(8,128)(2,1)}) %all-gather.2.cloned.1.call-update) | async-done | bytes 3145744 | tf_op jit(solution)/shard_map/all_gather | solution.py:32
  90.0 9.8 %fusion.25 = f32[1024,1536]{1,0:T(8,128)} fusion(bf16[1024,1536]{1,0:T(8,128)(2,1)} %all-gather.2.cloned.1.call-done, bf16[1536,1536]{1,0:T(8,128)(2,1)} %param.5), kind=kOutput, calls=%fused_computation.53 | convolution fusion | flops 4831838208 | bytes 14155776 | tf_op jit(solution)/shard_map/dot_general | solution.py:40
  99.7 0.0 reduce-scatter.2.cloned.1.call-update
  99.7 1.0 copy-done
  100.7 5.6 %collective-permute-start = (bf16[128,1536]{1,0:T(8,128)(2,1)S(1)}, bf16[128,1536]{1,0:T(8,128)(2,1)S(1)}, u32[]{:S(2)}, u32[]{:S(2)}) collective-permute-start(bf16[128,1536]{1,0:T(8,128)(2,1)S(1)} %copy-done), channel_id=1, source_target_pairs={{0,1},{1,2},{2,3},{3,4},{4,5},{5,6},{6,7},{7,0},{8,9},{9,10},{10,1... | collective-permute-start | bytes 1179656 | tf_op jit(solution)/shard_map/ppermute | solution.py:14
  106.4 4.7 %collective-permute-done = bf16[128,1536]{1,0:T(8,128)(2,1)S(1)} collective-permute-done((bf16[128,1536]{1,0:T(8,128)(2,1)S(1)}, bf16[128,1536]{1,0:T(8,128)(2,1)S(1)}, u32[]{:S(2)}, u32[]{:S(2)}) %collective-permute-start) | collective-permute-done | bytes 393248 | tf_op jit(solution)/shard_map/ppermute | solution.py:14
  111.1 2.5 %collective-permute-start.1 = (bf16[128,1536]{1,0:T(8,128)(2,1)S(1)}, bf16[128,1536]{1,0:T(8,128)(2,1)S(1)}, u32[]{:S(2)}, u32[]{:S(2)}) collective-permute-start(bf16[128,1536]{1,0:T(8,128)(2,1)S(1)} %collective-permute-done), channel_id=1, source_target_pairs={{0,1},{1,2},{2,3},{3,4},{4,5},{5,6},{6,7},{7,0},{8,9},{9,10},{10,1... | collective-permute-start | bytes 1179656 | tf_op jit(solution)/shard_map/ppermute | solution.py:14
  113.6 0.1 collective-permute-start.4
  113.7 8.9 %collective-permute-done.1 = bf16[128,1536]{1,0:T(8,128)(2,1)S(1)} collective-permute-done((bf16[128,1536]{1,0:T(8,128)(2,1)S(1)}, bf16[128,1536]{1,0:T(8,128)(2,1)S(1)}, u32[]{:S(2)}, u32[]{:S(2)}) %collective-permute-start.1) | collective-permute-done | bytes 393248 | tf_op jit(solution)/shard_map/ppermute | solution.py:14
  122.6 2.5 %collective-permute-start.2 = (bf16[128,1536]{1,0:T(8,128)(2,1)S(1)}, bf16[128,1536]{1,0:T(8,128)(2,1)S(1)}, u32[]{:S(2)}, u32[]{:S(2)}) collective-permute-start(bf16[128,1536]{1,0:T(8,128)(2,1)S(1)} %collective-permute-done.1), channel_id=1, source_target_pairs={{0,1},{1,2},{2,3},{3,4},{4,5},{5,6},{6,7},{7,0},{8,9},{9,10},{10,1... | collective-permute-start | bytes 1179656 | tf_op jit(solution)/shard_map/ppermute | solution.py:14
  125.0 0.4 collective-permute-done.4
  125.4 1.0 collective-permute-start.5
  126.4 7.6 %collective-permute-done.2 = bf16[128,1536]{1,0:T(8,128)(2,1)S(1)} collective-permute-done((bf16[128,1536]{1,0:T(8,128)(2,1)S(1)}, bf16[128,1536]{1,0:T(8,128)(2,1)S(1)}, u32[]{:S(2)}, u32[]{:S(2)}) %collective-permute-start.2) | collective-permute-done | bytes 393248 | tf_op jit(solution)/shard_map/ppermute | solution.py:14
  134.0 2.5 %collective-permute-start.3 = (bf16[128,1536]{1,0:T(8,128)(2,1)S(1)}, bf16[128,1536]{1,0:T(8,128)(2,1)S(1)}, u32[]{:S(2)}, u32[]{:S(2)}) collective-permute-start(bf16[128,1536]{1,0:T(8,128)(2,1)S(1)} %collective-permute-done.2), channel_id=1, source_target_pairs={{0,1},{1,2},{2,3},{3,4},{4,5},{5,6},{6,7},{7,0},{8,9},{9,10},{10,1... | collective-permute-start | bytes 1179656 | tf_op jit(solution)/shard_map/ppermute | solution.py:14
  136.5 0.8 collective-permute-done.5
  137.3 1.8 %collective-permute-start.6 = (bf16[128,1536]{1,0:T(8,128)(2,1)S(1)}, bf16[128,1536]{1,0:T(8,128)(2,1)S(1)}, u32[]{:S(2)}, u32[]{:S(2)}) collective-permute-start(bf16[128,1536]{1,0:T(8,128)(2,1)S(1)} %collective-permute-done.5), channel_id=1, source_target_pairs={{0,7},{1,0},{2,1},{3,2},{4,3},{5,4},{6,5},{7,6},{8,15},{9,8},{10,9... | collective-permute-start | bytes 1179656 | tf_op jit(solution)/shard_map/ppermute | solution.py:16
  139.1 6.4 %collective-permute-done.3 = bf16[128,1536]{1,0:T(8,128)(2,1)S(1)} collective-permute-done((bf16[128,1536]{1,0:T(8,128)(2,1)S(1)}, bf16[128,1536]{1,0:T(8,128)(2,1)S(1)}, u32[]{:S(2)}, u32[]{:S(2)}) %collective-permute-start.3) | collective-permute-done | bytes 393248 | tf_op jit(solution)/shard_map/ppermute | solution.py:14
  145.8 3.4 %collective-permute-done.6 = bf16[128,1536]{1,0:T(8,128)(2,1)S(1)} collective-permute-done((bf16[128,1536]{1,0:T(8,128)(2,1)S(1)}, bf16[128,1536]{1,0:T(8,128)(2,1)S(1)}, u32[]{:S(2)}, u32[]{:S(2)}) %collective-permute-start.6) | collective-permute-done | bytes 393248 | tf_op jit(solution)/shard_map/ppermute | solution.py:16
  149.5 7.4 %convolution_convert_fusion = bf16[1536,1536]{1,0:T(8,128)(2,1)} fusion(bf16[1024,1536]{1,0:T(8,128)(2,1)S(1)} %copy-done.1, bf16[2048,1536]{1,0:T(8,128)(2,1)S(1)} %constant_dynamic-update-slice_fusion, s32[]{:T(128)S(6)} %select_n.14), kind=kOutput, calls=%fused_computation.5 | convolution fusion | flops 4849926144 | bytes 11010052 | tf_op jit(solution)/shard_map/dot_general | solution.py:36
  156.9 0.7 reduce-scatter.2.cloned.1.call-done
  157.6 2.4 %fusion.18 = bf16[128,1536]{1,0:T(8,128)(2,1)} fusion(f32[128,1536]{1,0:T(8,128)} %reduce-scatter.2.cloned.1.call-done, bf16[128,1536]{1,0:T(8,128)(2,1)S(1)} %copy-done), kind=kLoop, calls=%fused_computation.30 | loop fusion | flops 3932160 | bytes 1572864 | tf_op jit(solution)/shard_map/convert_element_type | solution.py:48
  (19 shorter events, 0.4 us)
Async XLA Ops:
  7.2 82.8 %all-gather.2.cloned.1.call-start = ((), (), s32[]{:S(2)}) async-start(), calls=%async_computation.1 | async-start | bytes 3244032 | tf_op jit(solution)/shard_map/all_gather | solution.py:32
  7.9 149.7 %reduce-scatter.2.cloned.1.call-start = ((), (), s32[]{:S(2)}) async-start(), calls=%async_computation.2 | async-start | bytes 7077888 | tf_op jit(solution)/shard_map/reduce_scatter | solution.py:39
  99.7 1.0 copy-start
  100.7 10.4 %collective-permute-start = (bf16[128,1536]{1,0:T(8,128)(2,1)S(1)}, bf16[128,1536]{1,0:T(8,128)(2,1)S(1)}, u32[]{:S(2)}, u32[]{:S(2)}) collective-permute-start(bf16[128,1536]{1,0:T(8,128)(2,1)S(1)} %copy-done), channel_id=1, source_target_pairs={{0,1},{1,2},{2,3},{3,4},{4,5},{5,6},{6,7},{7,0},{8,9},{9,10},{10,1... | collective-permute-start | bytes 1179656 | tf_op jit(solution)/shard_map/ppermute | solution.py:14
  111.1 11.5 %collective-permute-start.1 = (bf16[128,1536]{1,0:T(8,128)(2,1)S(1)}, bf16[128,1536]{1,0:T(8,128)(2,1)S(1)}, u32[]{:S(2)}, u32[]{:S(2)}) collective-permute-start(bf16[128,1536]{1,0:T(8,128)(2,1)S(1)} %collective-permute-done), channel_id=1, source_target_pairs={{0,1},{1,2},{2,3},{3,4},{4,5},{5,6},{6,7},{7,0},{8,9},{9,10},{10,1... | collective-permute-start | bytes 1179656 | tf_op jit(solution)/shard_map/ppermute | solution.py:14
  113.6 11.9 %collective-permute-start.4 = (bf16[128,1536]{1,0:T(8,128)(2,1)S(1)}, bf16[128,1536]{1,0:T(8,128)(2,1)S(1)}, u32[]{:S(2)}, u32[]{:S(2)}) collective-permute-start(bf16[128,1536]{1,0:T(8,128)(2,1)S(1)} %copy-done), channel_id=1, source_target_pairs={{0,7},{1,0},{2,1},{3,2},{4,3},{5,4},{6,5},{7,6},{8,15},{9,8},{10,9... | collective-permute-start | bytes 1179656 | tf_op jit(solution)/shard_map/ppermute | solution.py:16
  122.6 11.5 %collective-permute-start.2 = (bf16[128,1536]{1,0:T(8,128)(2,1)S(1)}, bf16[128,1536]{1,0:T(8,128)(2,1)S(1)}, u32[]{:S(2)}, u32[]{:S(2)}) collective-permute-start(bf16[128,1536]{1,0:T(8,128)(2,1)S(1)} %collective-permute-done.1), channel_id=1, source_target_pairs={{0,1},{1,2},{2,3},{3,4},{4,5},{5,6},{6,7},{7,0},{8,9},{9,10},{10,1... | collective-permute-start | bytes 1179656 | tf_op jit(solution)/shard_map/ppermute | solution.py:14
  125.4 11.9 %collective-permute-start.5 = (bf16[128,1536]{1,0:T(8,128)(2,1)S(1)}, bf16[128,1536]{1,0:T(8,128)(2,1)S(1)}, u32[]{:S(2)}, u32[]{:S(2)}) collective-permute-start(bf16[128,1536]{1,0:T(8,128)(2,1)S(1)} %collective-permute-done.4), channel_id=1, source_target_pairs={{0,7},{1,0},{2,1},{3,2},{4,3},{5,4},{6,5},{7,6},{8,15},{9,8},{10,9... | collective-permute-start | bytes 1179656 | tf_op jit(solution)/shard_map/ppermute | solution.py:16
  134.0 11.5 %collective-permute-start.3 = (bf16[128,1536]{1,0:T(8,128)(2,1)S(1)}, bf16[128,1536]{1,0:T(8,128)(2,1)S(1)}, u32[]{:S(2)}, u32[]{:S(2)}) collective-permute-start(bf16[128,1536]{1,0:T(8,128)(2,1)S(1)} %collective-permute-done.2), channel_id=1, source_target_pairs={{0,1},{1,2},{2,3},{3,4},{4,5},{5,6},{6,7},{7,0},{8,9},{9,10},{10,1... | collective-permute-start | bytes 1179656 | tf_op jit(solution)/shard_map/ppermute | solution.py:14
  136.5 13.0 %copy-start.1 = (bf16[1024,1536]{1,0:T(8,128)(2,1)S(1)}, bf16[1024,1536]{1,0:T(8,128)(2,1)}, u32[]{:S(2)}) copy-start(bf16[1024,1536]{1,0:T(8,128)(2,1)} %all-gather.2.cloned.1.call-done) | copy-start | bytes 9437188
  137.3 11.9 %collective-permute-start.6 = (bf16[128,1536]{1,0:T(8,128)(2,1)S(1)}, bf16[128,1536]{1,0:T(8,128)(2,1)S(1)}, u32[]{:S(2)}, u32[]{:S(2)}) collective-permute-start(bf16[128,1536]{1,0:T(8,128)(2,1)S(1)} %collective-permute-done.5), channel_id=1, source_target_pairs={{0,7},{1,0},{2,1},{3,2},{4,3},{5,4},{6,5},{7,6},{8,15},{9,8},{10,9... | collective-permute-start | bytes 1179656 | tf_op jit(solution)/shard_map/ppermute | solution.py:16
Sparse Core Ops, SparseCore 0:
  10.5 79.3 all-gather.1
  99.9 57.6 reduce-scatter.1
